TPU v7x, 512 devices: a whole 4x8x8 slice. The times are simulated.
512 devices in a mesh: feat: 16 (over x, z_hi, core), samp: 32 (over y, z_lo).
Axes of the slice: x: 4, y: 8, z: 8 (z_hi: 2, z_lo: 4; z = z_hi * 4 + z_lo), core: 2. Of those that a mesh axis runs over, the one named last changes fastest.
Arguments:
- tier_one: bfloat16 [8192, 12288], P('feat', 'samp')
- residuals: bfloat16 [12288, 128], P('samp'), may hold values from -6 to 6
- pair_list: int32 [3, 65536], P(None, 'feat'), may hold values from 0 to 8191, as said below
Outputs:
- scores: float32 [65536, 128], P(('feat', 'samp'))
Inputs may be any that keep to these rules, and one draw needn't show every extreme that they name: `pair_list`: rows 0 and 1 are feature indices, row 2 an operator id of 0 to 3; each descriptor's two features differ.
All inputs are finite; a program needn't handle non-finite values.
Results may differ from a plain program's by a relative error of at most 0.0031.
Values may be sent and summed in bfloat16 or wider, within the bound.
No kernel may reach another device: no remote copies, remote signals or barrier semaphores. Data moves between devices by JAX's collectives and lax.ppermute only.
A program may use at most 64 MiB of HBM per device.

v0:
```python
import math
import jax
import jax.numpy as jnp
import numpy as np
from jax import lax
from jax.sharding import Mesh
from jax.sharding import PartitionSpec as P

epsilon = 1e-05
FEAT_AXES = ("x", "zh", "c")
SAMP_AXES = ("y", "zl")
EXTRA_ROWS = 16


def combine_rows(first_rows, second_rows, operator_id):
    first_rows = first_rows.astype(jnp.float32)
    second_rows = second_rows.astype(jnp.float32)
    quotient = first_rows / (1.0 + jnp.abs(second_rows))
    built = jnp.where(
        operator_id == 0,
        first_rows + second_rows,
        jnp.where(
            operator_id == 1,
            first_rows - second_rows,
            jnp.where(operator_id == 2, first_rows * second_rows, quotient),
        ),
    )
    return built.astype(jnp.bfloat16)


def ring_gather(block, axis, n):
    assert n == 4
    fwd = [(i, (i + 1) % n) for i in range(n)]
    bwd = [(i, (i - 1) % n) for i in range(n)]
    from_left = lax.ppermute(block, axis, perm=fwd)
    from_right = lax.ppermute(block, axis, perm=bwd)
    half = block.shape[0] // 2
    far_a = lax.ppermute(from_left[:half], axis, perm=fwd)
    far_b = lax.ppermute(from_right[half:], axis, perm=bwd)
    return jnp.concatenate([block, from_right, far_a, far_b, from_left], axis=0)


def split3(v):
    hi = lax.reduce_precision(v, exponent_bits=8, mantissa_bits=7)
    rest = v - hi
    mid = lax.reduce_precision(rest, exponent_bits=8, mantissa_bits=7)
    lo = rest - mid
    return jnp.stack([hi, mid, lo], axis=-2).astype(jnp.bfloat16)


def finish(product, first_sums, square_sums, col_totals, sample_count):
    means = first_sums / sample_count
    variance = square_sums / sample_count - means * means
    centred = product - means[:, None] * col_totals[None, :]
    return centred * lax.rsqrt(variance + epsilon)[:, None] / math.sqrt(sample_count)


def per_device(tier_one, residuals, pair_list):
    local_rows = tier_one.shape[0]
    local_pairs = pair_list.shape[1]
    width_k = residuals.shape[1]
    n_x = lax.axis_size("x")
    n_zh = lax.axis_size("zh")
    n_y = lax.axis_size("y")
    n_zl = lax.axis_size("zl")
    n_samp = n_y * n_zl
    sample_count = residuals.shape[0] * n_samp
    rows = lax.all_gather(tier_one, "zh", axis=0, tiled=True)
    rows = ring_gather(rows, "x", n_x)
    other = lax.ppermute(rows, "c", perm=[(0, 1), (1, 0)])
    rows = jnp.concatenate([rows, other], axis=0)
    my_c = lax.axis_index("c")
    my_x = lax.axis_index("x")

    def position(g):
        f, r = (g // local_rows, g % local_rows)
        x, zh, c = (f // (2 * n_zh), f // 2 % n_zh, f % 2)
        half = (c != my_c).astype(jnp.int32)
        x_slot = (x - my_x + n_x) % n_x
        return ((half * n_x + x_slot) * n_zh + zh) * local_rows + r

    first = jnp.take(rows, position(pair_list[0]), axis=0)
    second = jnp.take(rows, position(pair_list[1]), axis=0)
    built = combine_rows(first, second, pair_list[2][:, None])
    product = jnp.dot(built, residuals, preferred_element_type=jnp.float32)
    widened = built.astype(jnp.float32)
    first_sums = jnp.sum(widened, axis=1)
    square_sums = jnp.sum(widened * widened, axis=1)
    col_part = jnp.sum(residuals.astype(jnp.float32), axis=0)
    local_samples = residuals.shape[0]
    local_means = first_sums / local_samples
    centred = product - local_means[:, None] * col_part[None, :]
    blocks = local_pairs // width_k
    block_rows = width_k + EXTRA_ROWS
    extras = jnp.concatenate(
        [
            split3(jnp.broadcast_to(col_part[None, :], (blocks, width_k))),
            split3(first_sums.reshape(blocks, width_k)),
            split3(square_sums.reshape(blocks, width_k)),
            jnp.zeros((blocks, EXTRA_ROWS - 9, width_k), jnp.bfloat16),
        ],
        axis=1,
    )
    packed = jnp.concatenate(
        [centred.astype(jnp.bfloat16).reshape(blocks, width_k, width_k), extras], axis=1
    )
    arrived = lax.all_to_all(packed, SAMP_AXES, 0, 0, tiled=False)
    centred_sum = jnp.sum(arrived[:, :width_k].astype(jnp.float32), axis=0)
    pieces = arrived[:, width_k:].astype(jnp.float32)

    def joined(i):
        return pieces[:, i] + pieces[:, i + 1] + pieces[:, i + 2]

    col_parts, first_parts, square_parts = (joined(0), joined(3), joined(6))
    mean_share = jnp.einsum(
        "dp,dk->pk", first_parts / local_samples, col_parts, precision=lax.Precision.HIGHEST
    )
    return finish(
        centred_sum + mean_share,
        jnp.sum(first_parts, axis=0),
        jnp.sum(square_parts, axis=0),
        jnp.sum(col_parts, axis=0),
        sample_count,
    )


def solution(mesh):
    n_feat, n_samp = mesh.devices.shape
    n_c, n_zh = (2, 2)
    n_x = n_feat // (n_c * n_zh)
    n_zl = 4
    n_y = n_samp // n_zl
    devices = np.asarray(mesh.devices).reshape(n_x, n_zh, n_c, n_y, n_zl)
    fine = Mesh(devices, FEAT_AXES + SAMP_AXES)
    in_specs = (P(FEAT_AXES, SAMP_AXES), P(SAMP_AXES, None), P(None, FEAT_AXES))
    out_specs = P(FEAT_AXES + SAMP_AXES, None)
    return jax.shard_map(
        per_device, mesh=fine, in_specs=in_specs, out_specs=out_specs, check_vma=False
    )
```

profile of v0, /device:TPU:6, one launch (start us, length us, event | category | flops | bytes accessed | tf_op | source)
XLA Modules:
  0.0 170.4 jit_solution(11472657003874128858)
XLA Ops:
  0.0 19.2 %all_gather.3 = bf16[1024,384]{1,0:T(8,128)(2,1)S(1)} all-gather(bf16[512,384]{1,0:T(8,128)(2,1)} %param.5), channel_id=1, replica_groups=mesh['x'=4,'zh'=2,'c'=2,'y'=8,'zl'=4] {'zh'}, dimensions={0}, use_global_device_ids=true | all-gather | bytes 1179648 | tf_op jit(solution)/shard_map/all_gather | solution.py:68
  19.2 2.4 %collective-permute-start.1 = (bf16[1024,384]{1,0:T(8,128)(2,1)S(1)}, bf16[1024,384]{1,0:T(8,128)(2,1)S(1)}, u32[]{:S(2)}, u32[]{:S(2)}) collective-permute-start(bf16[1024,384]{1,0:T(8,128)(2,1)S(1)} %all_gather.3), channel_id=1, source_target_pairs={{0,128},{128,256},{256,384},{384,0},{1,129},{129,257},{257,385},{3... | collective-permute-start | bytes 2359304 | tf_op jit(solution)/shard_map/ppermute | solution.py:35
  21.6 3.5 %collective-permute-start = (bf16[1024,384]{1,0:T(8,128)(2,1)S(1)}, bf16[1024,384]{1,0:T(8,128)(2,1)S(1)}, u32[]{:S(2)}, u32[]{:S(2)}) collective-permute-start(bf16[1024,384]{1,0:T(8,128)(2,1)S(1)} %all_gather.3), channel_id=1, source_target_pairs={{0,384},{128,0},{256,128},{384,256},{1,385},{129,1},{257,129},{385... | collective-permute-start | bytes 2359304 | tf_op jit(solution)/shard_map/ppermute | solution.py:36
  25.0 14.7 %collective-permute-done.1 = bf16[1024,384]{1,0:T(8,128)(2,1)S(1)} collective-permute-done((bf16[1024,384]{1,0:T(8,128)(2,1)S(1)}, bf16[1024,384]{1,0:T(8,128)(2,1)S(1)}, u32[]{:S(2)}, u32[]{:S(2)}) %collective-permute-start.1) | collective-permute-done | bytes 786464 | tf_op jit(solution)/shard_map/ppermute | solution.py:35
  39.8 3.4 %collective-permute-start.2 = (bf16[512,384]{1,0:T(8,128)(2,1)S(1)}, bf16[512,384]{1,0:T(8,128)(2,1)S(1)}, u32[]{:S(2)}, u32[]{:S(2)}) collective-permute-start(bf16[512,384]{1,0:T(8,128)(2,1)S(1)} %slice.68), channel_id=1, source_target_pairs={{0,128},{128,256},{256,384},{384,0},{1,129},{129,257},{257,385},{3... | collective-permute-start | bytes 1179656 | tf_op jit(solution)/shard_map/ppermute | solution.py:38
  43.2 0.0 collective-permute-done
  43.3 2.4 %collective-permute-start.3 = (bf16[512,384]{1,0:T(8,128)(2,1)S(1)}, bf16[512,384]{1,0:T(8,128)(2,1)S(1)}, u32[]{:S(2)}, u32[]{:S(2)}) collective-permute-start(bf16[512,384]{1,0:T(8,128)(2,1)S(1)} %slice.69), channel_id=1, source_target_pairs={{0,384},{128,0},{256,128},{384,256},{1,385},{129,1},{257,129},{385... | collective-permute-start | bytes 1179656 | tf_op jit(solution)/shard_map/ppermute | solution.py:39
  45.7 1.3 constant_dynamic-update-slice_fusion.4
  47.0 0.0 copy-start
  47.0 1.3 constant_dynamic-update-slice_fusion.3
  48.3 2.7 %collective-permute-done.2 = bf16[512,384]{1,0:T(8,128)(2,1)S(1)} collective-permute-done((bf16[512,384]{1,0:T(8,128)(2,1)S(1)}, bf16[512,384]{1,0:T(8,128)(2,1)S(1)}, u32[]{:S(2)}, u32[]{:S(2)}) %collective-permute-start.2) | collective-permute-done | bytes 393248 | tf_op jit(solution)/shard_map/ppermute | solution.py:38
  51.0 1.0 constant_dynamic-update-slice_fusion.2
  52.0 3.2 %collective-permute-done.3 = bf16[512,384]{1,0:T(8,128)(2,1)S(1)} collective-permute-done((bf16[512,384]{1,0:T(8,128)(2,1)S(1)}, bf16[512,384]{1,0:T(8,128)(2,1)S(1)}, u32[]{:S(2)}, u32[]{:S(2)}) %collective-permute-start.3) | collective-permute-done | bytes 393248 | tf_op jit(solution)/shard_map/ppermute | solution.py:39
  55.2 1.0 constant_dynamic-update-slice_fusion.1
  56.3 1.3 constant_dynamic-update-slice_fusion
  57.6 1.9 %collective-permute-start.4 = (bf16[4096,384]{1,0:T(8,128)(2,1)}, bf16[4096,384]{1,0:T(8,128)(2,1)S(1)}, u32[]{:S(2)}, u32[]{:S(2)}) collective-permute-start(bf16[4096,384]{1,0:T(8,128)(2,1)} %get-tuple-element.20), channel_id=1, source_target_pairs={{0,32},{32,0},{1,33},{33,1},{2,34},{34,2},{3,35},{35,3},{4,36},{36... | collective-permute-start | bytes 9437192 | tf_op jit(solution)/shard_map/ppermute | solution.py:70
  59.5 0.0 copy-done
  59.5 0.1 convert_reduce_fusion.2
  59.6 0.0 copy-done.1
  59.6 0.2 compare_reduce_fusion.2
  59.8 0.1 compare_and_fusion
  60.0 5.4 %collective-permute-done.4 = bf16[4096,384]{1,0:T(8,128)(2,1)S(1)} collective-permute-done((bf16[4096,384]{1,0:T(8,128)(2,1)}, bf16[4096,384]{1,0:T(8,128)(2,1)S(1)}, u32[]{:S(2)}, u32[]{:S(2)}) %collective-permute-start.4) | collective-permute-done | bytes 3145760 | tf_op jit(solution)/shard_map/ppermute | solution.py:70
  65.4 2.0 %constant_dynamic-update-slice_fusion.5 = bf16[8192,384]{1,0:T(8,128)(2,1)} fusion(bf16[8192,384]{1,0:T(8,128)(2,1)} %get-tuple-element.21, bf16[4096,384]{1,0:T(8,128)(2,1)S(1)} %collective-permute-done.4), kind=kLoop, calls=%fused_computation.80 | loop fusion | bytes 6291456 | tf_op jit(solution)/shard_map/concatenate | solution.py:71
  67.4 17.6 %gather_fusion = bf16[4096,384]{1,0:T(8,128)(2,1)S(1)} fusion(bf16[8192,384]{1,0:T(8,128)(2,1)} %constant_dynamic-update-slice_fusion.5, s32[4096]{0:T(1024)S(1)} %broadcast_clamp_fusion.1), kind=kCustom, calls=%fused_computation.clone | custom fusion | bytes 6307840 | tf_op jit(solution)/shard_map/jit(_take)/gather | solution.py:82
  85.0 20.3 %gather_fusion.1 = bf16[4096,384]{1,0:T(8,128)(2,1)} fusion(bf16[8192,384]{1,0:T(8,128)(2,1)} %constant_dynamic-update-slice_fusion.5, s32[4096]{0:T(1024)S(1)} %broadcast_clamp_fusion), kind=kCustom, calls=%fused_computation.1.clone | custom fusion | bytes 6307840 | tf_op jit(solution)/shard_map/jit(_take)/gather | solution.py:83
  105.3 8.6 %fusion = (f32[4096]{0:T(1024)S(1)}, f32[4096]{0:T(1024)S(1)}, bf16[4096,384]{1,0:T(8,128)(2,1)S(1)}) fusion(pred[4096]{0:T(1024)(128)(4,1)S(1)} %get-tuple-element.10, pred[4096]{0:T(1024)(128)(4,1)S(1)} %get-tuple-element.9, bf16[4096,384]{1,0:T(8,128)(2,1)} %gather_fusion.1, pred[4096]{0:T(1024)(128)(4,1)S(1)} %get-tuple-element.18, ...), kind=kLoop, calls=%fused_computation.9 | loop fusion | flops 28303360 | bytes 9490432 | tf_op jit(solution)/shard_map/reduce_sum | solution.py:88
  114.1 1.2 fusion.6
  115.4 0.6 concatenate.13
  116.0 53.1 %all_to_all.5 = bf16[32,144,128]{2,1,0:T(8,128)(2,1)S(1)} all-to-all(bf16[32,144,128]{2,1,0:T(8,128)(2,1)S(1)} %concatenate.13), channel_id=1, replica_groups=mesh['x'=4,'zh'=2,'c'=2,'y'=8,'zl'=4] {'y','zl'}, dimensions={0} | all-to-all | bytes 2359296 | tf_op jit(solution)/shard_map/all_to_all | solution.py:107
  169.1 0.1 fusion.42
  169.3 0.2 convert_reduce_fusion.1
  169.5 0.9 fusion.9
  (23 shorter events, 0.3 us)
Async XLA Ops:
  19.2 20.6 %collective-permute-start.1 = (bf16[1024,384]{1,0:T(8,128)(2,1)S(1)}, bf16[1024,384]{1,0:T(8,128)(2,1)S(1)}, u32[]{:S(2)}, u32[]{:S(2)}) collective-permute-start(bf16[1024,384]{1,0:T(8,128)(2,1)S(1)} %all_gather.3), channel_id=1, source_target_pairs={{0,128},{128,256},{256,384},{384,0},{1,129},{129,257},{257,385},{3... | collective-permute-start | bytes 2359304 | tf_op jit(solution)/shard_map/ppermute | solution.py:35
  21.6 21.6 %collective-permute-start = (bf16[1024,384]{1,0:T(8,128)(2,1)S(1)}, bf16[1024,384]{1,0:T(8,128)(2,1)S(1)}, u32[]{:S(2)}, u32[]{:S(2)}) collective-permute-start(bf16[1024,384]{1,0:T(8,128)(2,1)S(1)} %all_gather.3), channel_id=1, source_target_pairs={{0,384},{128,0},{256,128},{384,256},{1,385},{129,1},{257,129},{385... | collective-permute-start | bytes 2359304 | tf_op jit(solution)/shard_map/ppermute | solution.py:36
  39.8 11.2 %collective-permute-start.2 = (bf16[512,384]{1,0:T(8,128)(2,1)S(1)}, bf16[512,384]{1,0:T(8,128)(2,1)S(1)}, u32[]{:S(2)}, u32[]{:S(2)}) collective-permute-start(bf16[512,384]{1,0:T(8,128)(2,1)S(1)} %slice.68), channel_id=1, source_target_pairs={{0,128},{128,256},{256,384},{384,0},{1,129},{129,257},{257,385},{3... | collective-permute-start | bytes 1179656 | tf_op jit(solution)/shard_map/ppermute | solution.py:38
  43.3 12.0 %collective-permute-start.3 = (bf16[512,384]{1,0:T(8,128)(2,1)S(1)}, bf16[512,384]{1,0:T(8,128)(2,1)S(1)}, u32[]{:S(2)}, u32[]{:S(2)}) collective-permute-start(bf16[512,384]{1,0:T(8,128)(2,1)S(1)} %slice.69), channel_id=1, source_target_pairs={{0,384},{128,0},{256,128},{384,256},{1,385},{129,1},{257,129},{385... | collective-permute-start | bytes 1179656 | tf_op jit(solution)/shard_map/ppermute | solution.py:39
  47.0 12.5 %copy-start = (bf16[384,128]{1,0:T(8,128)(2,1)S(1)}, bf16[384,128]{1,0:T(8,128)(2,1)}, u32[]{:S(2)}) copy-start(bf16[384,128]{1,0:T(8,128)(2,1)} %param.6) | copy-start | bytes 294916
  47.0 12.6 %copy-start.1 = (s32[3,4096]{1,0:T(4,128)S(1)}, s32[3,4096]{1,0:T(4,128)}, u32[]{:S(2)}) copy-start(s32[3,4096]{1,0:T(4,128)} %param.7) | copy-start | bytes 147460
  57.6 7.8 %collective-permute-start.4 = (bf16[4096,384]{1,0:T(8,128)(2,1)}, bf16[4096,384]{1,0:T(8,128)(2,1)S(1)}, u32[]{:S(2)}, u32[]{:S(2)}) collective-permute-start(bf16[4096,384]{1,0:T(8,128)(2,1)} %get-tuple-element.20), channel_id=1, source_target_pairs={{0,32},{32,0},{1,33},{33,1},{2,34},{34,2},{3,35},{35,3},{4,36},{36... | collective-permute-start | bytes 9437192 | tf_op jit(solution)/shard_map/ppermute | solution.py:70
where the time goes:
time: 171 us; the launch traced here: 170 us
  blocking collectives  72.3 us (42%)
  local copies, waits for them, and re-layouts  46.7 us (27%)
  waiting for transfers between devices  26.1 us (15%)
  starting transfers between devices  13.6 us (8%)
  other arithmetic  9.33 us (5%)
  matrix products  2.11 us (1%)
    all_to_all x1, blocking collectives, per_device(): arrived = lax.all_to_all(packed, SAMP_AXES, 0, 0, tiled=False)  53.1 us
    gather x1, local copies, waits for them, and re-layouts, per_device(): second = jnp.take(rows, position(pair_list[1]), axis=0)  20.3 us
    all_gather x1, blocking collectives, per_device(): rows = lax.all_gather(tier_one, 'zh', axis=0, tiled=True)  19.2 us
    gather x1, local copies, waits for them, and re-layouts, per_device(): first = jnp.take(rows, position(pair_list[0]), axis=0)  17.6 us
    ppermute x1, waiting for transfers between devices, ring_gather(): from_left = lax.ppermute(block, axis, perm=fwd)  14.7 us
    reduce_sum x1, other arithmetic, per_device(): square_sums = jnp.sum(widened * widened, axis=1)  8.61 us
    ppermute x1, waiting for transfers between devices, per_device(): other = lax.ppermute(rows, 'c', perm=[(0, 1), (1, 0)])  5.39 us
    unnamed x8, local copies, waits for them, and re-layouts  4.57 us
  transfers between devices with their start and end apart: 5, of which 4 were waited for; matrix products, arithmetic and copies ran while one was open for 2% of the time, Pallas kernels for 0%

commit v1 on v0

--- a/solution.py
+++ b/solution.py
@@ -65,7 +65,9 @@
     n_zl = lax.axis_size("zl")
     n_samp = n_y * n_zl
     sample_count = residuals.shape[0] * n_samp
-    rows = lax.all_gather(tier_one, "zh", axis=0, tiled=True)
+    rows = jnp.concatenate(
+        lax.all_to_all(jnp.stack([tier_one] * lax.axis_size("zh")), "zh", 0, 0), axis=0
+    )
     rows = ring_gather(rows, "x", n_x)
     other = lax.ppermute(rows, "c", perm=[(0, 1), (1, 0)])
     rows = jnp.concatenate([rows, other], axis=0)

time: 171 us -> 178 us (1.041)
  blocking collectives: 72.3 us -> 81.3 us
  waiting for transfers between devices: 26.1 us -> 22.7 us
    all_to_all x0 -> x1, blocking collectives: none -> 33.2 us  [per_device(): lax.all_to_all(jnp.stack([tier_one] * lax.axis_size('zh')), 'zh', 0, 0)]
    all_gather x1 -> x0, blocking collectives: 19.2 us -> none  [per_device(): rows = lax.all_gather(tier_one, 'zh', axis=0, tiled=True)]
    all_to_all x1, blocking collectives: 53.1 us -> 48.1 us  [per_device(): arrived = lax.all_to_all(packed, SAMP_AXES, 0, 0, tiled=False)]
    ppermute x1, waiting for transfers between devices: 14.7 us -> 12.2 us  [ring_gather(): from_left = lax.ppermute(block, axis, perm=fwd)]
where the time goes in v1:
time: 178 us; the launch traced here: 177 us
  blocking collectives  81.3 us (46%)
  local copies, waits for them, and re-layouts  46.7 us (26%)
  waiting for transfers between devices  22.7 us (13%)
  starting transfers between devices  13.6 us (8%)
  other arithmetic  10.6 us (6%)
  matrix products  2.12 us (1%)
    all_to_all x1, blocking collectives, per_device(): arrived = lax.all_to_all(packed, SAMP_AXES, 0, 0, tiled=False)  48.1 us
    all_to_all x1, blocking collectives, per_device(): lax.all_to_all(jnp.stack([tier_one] * lax.axis_size('zh')), 'zh', 0, 0)  33.2 us
    gather x1, local copies, waits for them, and re-layouts, per_device(): second = jnp.take(rows, position(pair_list[1]), axis=0)  20.3 us
    gather x1, local copies, waits for them, and re-layouts, per_device(): first = jnp.take(rows, position(pair_list[0]), axis=0)  17.6 us
    ppermute x1, waiting for transfers between devices, ring_gather(): from_left = lax.ppermute(block, axis, perm=fwd)  12.2 us
    reduce_sum x1, other arithmetic, per_device(): square_sums = jnp.sum(widened * widened, axis=1)  8.61 us
    ppermute x1, waiting for transfers between devices, per_device(): other = lax.ppermute(rows, 'c', perm=[(0, 1), (1, 0)])  5.39 us
    unnamed x8, local copies, waits for them, and re-layouts  4.57 us
  transfers between devices with their start and end apart: 5, of which 4 were waited for; matrix products, arithmetic and copies ran while one was open for 2% of the time, Pallas kernels for 0%

profile of v1, /device:TPU:6, one launch (start us, length us, event | category | flops | bytes accessed | tf_op | source)
XLA Modules:
  0.0 177.3 jit_solution(853915937602880994)
XLA Ops:
  0.0 1.2 pad_maximum_fusion
  1.2 33.2 %all_to_all.10 = bf16[2,512,384]{2,1,0:T(8,128)(2,1)S(1)} all-to-all(bf16[2,512,384]{2,1,0:T(8,128)(2,1)S(1)} %pad_maximum_fusion), channel_id=1, replica_groups=mesh['x'=4,'zh'=2,'c'=2,'y'=8,'zl'=4] {'zh'}, dimensions={0} | all-to-all | bytes 1572864 | tf_op jit(solution)/shard_map/all_to_all | solution.py:69
  34.4 2.4 %collective-permute-start.1 = (bf16[1024,384]{1,0:T(8,128)(2,1)S(1)}, bf16[1024,384]{1,0:T(8,128)(2,1)S(1)}, u32[]{:S(2)}, u32[]{:S(2)}) collective-permute-start(bf16[1024,384]{1,0:T(8,128)(2,1)S(1)} %bitcast.25), channel_id=1, source_target_pairs={{0,128},{128,256},{256,384},{384,0},{1,129},{129,257},{257,385},{3... | collective-permute-start | bytes 2359304 | tf_op jit(solution)/shard_map/ppermute | solution.py:35
  36.8 3.5 %collective-permute-start = (bf16[1024,384]{1,0:T(8,128)(2,1)S(1)}, bf16[1024,384]{1,0:T(8,128)(2,1)S(1)}, u32[]{:S(2)}, u32[]{:S(2)}) collective-permute-start(bf16[1024,384]{1,0:T(8,128)(2,1)S(1)} %bitcast.26), channel_id=1, source_target_pairs={{0,384},{128,0},{256,128},{384,256},{1,385},{129,1},{257,129},{385... | collective-permute-start | bytes 2359304 | tf_op jit(solution)/shard_map/ppermute | solution.py:36
  40.3 12.2 %collective-permute-done.1 = bf16[1024,384]{1,0:T(8,128)(2,1)S(1)} collective-permute-done((bf16[1024,384]{1,0:T(8,128)(2,1)S(1)}, bf16[1024,384]{1,0:T(8,128)(2,1)S(1)}, u32[]{:S(2)}, u32[]{:S(2)}) %collective-permute-start.1) | collective-permute-done | bytes 786464 | tf_op jit(solution)/shard_map/ppermute | solution.py:35
  52.6 3.6 %collective-permute-start.2 = (bf16[512,384]{1,0:T(8,128)(2,1)S(1)}, bf16[512,384]{1,0:T(8,128)(2,1)S(1)}, u32[]{:S(2)}, u32[]{:S(2)}) collective-permute-start(bf16[512,384]{1,0:T(8,128)(2,1)S(1)} %slice.68), channel_id=1, source_target_pairs={{0,128},{128,256},{256,384},{384,0},{1,129},{129,257},{257,385},{3... | collective-permute-start | bytes 1179656 | tf_op jit(solution)/shard_map/ppermute | solution.py:38
  56.2 0.0 collective-permute-done
  56.2 2.2 %collective-permute-start.3 = (bf16[512,384]{1,0:T(8,128)(2,1)S(1)}, bf16[512,384]{1,0:T(8,128)(2,1)S(1)}, u32[]{:S(2)}, u32[]{:S(2)}) collective-permute-start(bf16[512,384]{1,0:T(8,128)(2,1)S(1)} %slice.69), channel_id=1, source_target_pairs={{0,384},{128,0},{256,128},{384,256},{1,385},{129,1},{257,129},{385... | collective-permute-start | bytes 1179656 | tf_op jit(solution)/shard_map/ppermute | solution.py:39
  58.5 1.3 constant_dynamic-update-slice_fusion.4
  59.8 1.3 constant_dynamic-update-slice_fusion.3
  61.1 1.2 collective-permute-done.2
  62.2 1.0 constant_dynamic-update-slice_fusion.2
  63.2 3.9 %collective-permute-done.3 = bf16[512,384]{1,0:T(8,128)(2,1)S(1)} collective-permute-done((bf16[512,384]{1,0:T(8,128)(2,1)S(1)}, bf16[512,384]{1,0:T(8,128)(2,1)S(1)}, u32[]{:S(2)}, u32[]{:S(2)}) %collective-permute-start.3) | collective-permute-done | bytes 393248 | tf_op jit(solution)/shard_map/ppermute | solution.py:39
  67.1 1.0 constant_dynamic-update-slice_fusion.1
  68.1 1.3 constant_dynamic-update-slice_fusion
  69.5 1.9 %collective-permute-start.4 = (bf16[4096,384]{1,0:T(8,128)(2,1)}, bf16[4096,384]{1,0:T(8,128)(2,1)S(1)}, u32[]{:S(2)}, u32[]{:S(2)}) collective-permute-start(bf16[4096,384]{1,0:T(8,128)(2,1)} %get-tuple-element.20), channel_id=1, source_target_pairs={{0,32},{32,0},{1,33},{33,1},{2,34},{34,2},{3,35},{35,3},{4,36},{36... | collective-permute-start | bytes 9437192 | tf_op jit(solution)/shard_map/ppermute | solution.py:72
  71.4 0.0 copy-done
  71.4 0.1 convert_reduce_fusion.2
  71.5 0.0 copy-done.1
  71.5 0.2 compare_reduce_fusion.2
  71.7 0.1 compare_and_fusion
  71.8 5.4 %collective-permute-done.4 = bf16[4096,384]{1,0:T(8,128)(2,1)S(1)} collective-permute-done((bf16[4096,384]{1,0:T(8,128)(2,1)}, bf16[4096,384]{1,0:T(8,128)(2,1)S(1)}, u32[]{:S(2)}, u32[]{:S(2)}) %collective-permute-start.4) | collective-permute-done | bytes 3145760 | tf_op jit(solution)/shard_map/ppermute | solution.py:72
  77.2 2.0 %constant_dynamic-update-slice_fusion.5 = bf16[8192,384]{1,0:T(8,128)(2,1)} fusion(bf16[8192,384]{1,0:T(8,128)(2,1)} %get-tuple-element.21, bf16[4096,384]{1,0:T(8,128)(2,1)S(1)} %collective-permute-done.4), kind=kLoop, calls=%fused_computation.81 | loop fusion | bytes 6291456 | tf_op jit(solution)/shard_map/concatenate | solution.py:73
  79.2 17.6 %gather_fusion = bf16[4096,384]{1,0:T(8,128)(2,1)S(1)} fusion(bf16[8192,384]{1,0:T(8,128)(2,1)} %constant_dynamic-update-slice_fusion.5, s32[4096]{0:T(1024)S(1)} %broadcast_clamp_fusion.1), kind=kCustom, calls=%fused_computation.clone | custom fusion | bytes 6307840 | tf_op jit(solution)/shard_map/jit(_take)/gather | solution.py:84
  96.9 20.3 %gather_fusion.1 = bf16[4096,384]{1,0:T(8,128)(2,1)} fusion(bf16[8192,384]{1,0:T(8,128)(2,1)} %constant_dynamic-update-slice_fusion.5, s32[4096]{0:T(1024)S(1)} %broadcast_clamp_fusion), kind=kCustom, calls=%fused_computation.1.clone | custom fusion | bytes 6307840 | tf_op jit(solution)/shard_map/jit(_take)/gather | solution.py:85
  117.2 8.6 %fusion = (f32[4096]{0:T(1024)S(1)}, f32[4096]{0:T(1024)S(1)}, bf16[4096,384]{1,0:T(8,128)(2,1)S(1)}) fusion(pred[4096]{0:T(1024)(128)(4,1)S(1)} %get-tuple-element.10, pred[4096]{0:T(1024)(128)(4,1)S(1)} %get-tuple-element.9, bf16[4096,384]{1,0:T(8,128)(2,1)} %gather_fusion.1, pred[4096]{0:T(1024)(128)(4,1)S(1)} %get-tuple-element.18, ...), kind=kLoop, calls=%fused_computation.9 | loop fusion | flops 28303360 | bytes 9490432 | tf_op jit(solution)/shard_map/reduce_sum | solution.py:90
  126.0 1.2 fusion.6
  127.2 0.6 concatenate.13
  127.9 48.1 %all_to_all.11 = bf16[32,144,128]{2,1,0:T(8,128)(2,1)S(1)} all-to-all(bf16[32,144,128]{2,1,0:T(8,128)(2,1)S(1)} %concatenate.13), channel_id=1, replica_groups=mesh['x'=4,'zh'=2,'c'=2,'y'=8,'zl'=4] {'y','zl'}, dimensions={0} | all-to-all | bytes 2359296 | tf_op jit(solution)/shard_map/all_to_all | solution.py:109
  176.0 0.1 fusion.42
  176.2 0.2 convert_reduce_fusion.1
  176.3 0.9 fusion.9
  (24 shorter events, 0.3 us)
Async XLA Ops:
  34.4 18.1 %collective-permute-start.1 = (bf16[1024,384]{1,0:T(8,128)(2,1)S(1)}, bf16[1024,384]{1,0:T(8,128)(2,1)S(1)}, u32[]{:S(2)}, u32[]{:S(2)}) collective-permute-start(bf16[1024,384]{1,0:T(8,128)(2,1)S(1)} %bitcast.25), channel_id=1, source_target_pairs={{0,128},{128,256},{256,384},{384,0},{1,129},{129,257},{257,385},{3... | collective-permute-start | bytes 2359304 | tf_op jit(solution)/shard_map/ppermute | solution.py:35
  36.8 19.4 %collective-permute-start = (bf16[1024,384]{1,0:T(8,128)(2,1)S(1)}, bf16[1024,384]{1,0:T(8,128)(2,1)S(1)}, u32[]{:S(2)}, u32[]{:S(2)}) collective-permute-start(bf16[1024,384]{1,0:T(8,128)(2,1)S(1)} %bitcast.26), channel_id=1, source_target_pairs={{0,384},{128,0},{256,128},{384,256},{1,385},{129,1},{257,129},{385... | collective-permute-start | bytes 2359304 | tf_op jit(solution)/shard_map/ppermute | solution.py:36
  52.6 9.7 %collective-permute-start.2 = (bf16[512,384]{1,0:T(8,128)(2,1)S(1)}, bf16[512,384]{1,0:T(8,128)(2,1)S(1)}, u32[]{:S(2)}, u32[]{:S(2)}) collective-permute-start(bf16[512,384]{1,0:T(8,128)(2,1)S(1)} %slice.68), channel_id=1, source_target_pairs={{0,128},{128,256},{256,384},{384,0},{1,129},{129,257},{257,385},{3... | collective-permute-start | bytes 1179656 | tf_op jit(solution)/shard_map/ppermute | solution.py:38
  56.2 10.9 %collective-permute-start.3 = (bf16[512,384]{1,0:T(8,128)(2,1)S(1)}, bf16[512,384]{1,0:T(8,128)(2,1)S(1)}, u32[]{:S(2)}, u32[]{:S(2)}) collective-permute-start(bf16[512,384]{1,0:T(8,128)(2,1)S(1)} %slice.69), channel_id=1, source_target_pairs={{0,384},{128,0},{256,128},{384,256},{1,385},{129,1},{257,129},{385... | collective-permute-start | bytes 1179656 | tf_op jit(solution)/shard_map/ppermute | solution.py:39
  59.8 11.6 %copy-start = (bf16[384,128]{1,0:T(8,128)(2,1)S(1)}, bf16[384,128]{1,0:T(8,128)(2,1)}, u32[]{:S(2)}) copy-start(bf16[384,128]{1,0:T(8,128)(2,1)} %param.6) | copy-start | bytes 294916
  59.8 11.7 %copy-start.1 = (s32[3,4096]{1,0:T(4,128)S(1)}, s32[3,4096]{1,0:T(4,128)}, u32[]{:S(2)}) copy-start(s32[3,4096]{1,0:T(4,128)} %param.7) | copy-start | bytes 147460
  69.5 7.8 %collective-permute-start.4 = (bf16[4096,384]{1,0:T(8,128)(2,1)}, bf16[4096,384]{1,0:T(8,128)(2,1)S(1)}, u32[]{:S(2)}, u32[]{:S(2)}) collective-permute-start(bf16[4096,384]{1,0:T(8,128)(2,1)} %get-tuple-element.20), channel_id=1, source_target_pairs={{0,32},{32,0},{1,33},{33,1},{2,34},{34,2},{3,35},{35,3},{4,36},{36... | collective-permute-start | bytes 9437192 | tf_op jit(solution)/shard_map/ppermute | solution.py:72
